TPU v7x, 32 devices: a whole 2x2x4 slice. The times are simulated.
32 devices in a mesh: groups: 2 (over y), tm: 4 (over z), height: 2 (over x), chan: 2 (over core).
Axes of the slice: x: 2, y: 2, z: 4, core: 2. Of those that a mesh axis runs over, the one named last changes fastest.
Arguments:
- video: bfloat16 [16, 72, 320, 128], P(('groups', 'tm'), 'height', 'chan'), parts along dimension 0, may hold values from -52 to 52
- norm1_gain: float32 [320], P('chan'), may hold values from 0.25 to 1.75
- norm1_bias: float32 [320], P('chan'), may hold values from -3 to 3
- spatial_weight: bfloat16 [3, 3, 320, 320], P(None, None, 'tm', 'chan'), may hold values from -0.3125 to 0.3125
- spatial_bias: float32 [320], P('chan'), may hold values from -3 to 3
- norm2_gain: float32 [320], P('chan'), may hold values from 0.25 to 1.75
- norm2_bias: float32 [320], P('chan'), may hold values from -3 to 3
- temporal_weight: bfloat16 [3, 320, 320], P(None, 'tm', 'chan'), may hold values from -0.3125 to 0.3125
- temporal_bias: float32 [320], P('chan'), may hold values from -3 to 3
Outputs:
- clip_out: bfloat16 [16, 72, 320, 128], P(('groups', 'tm'), 'height', 'chan'), parts along dimension 0
There are 2 independent parts, one for each index of `groups`. A program takes and returns all parts, laid end to end along the dimension named above; an argument that names none is the same for every part. Nothing has to cross between parts.
All inputs are finite; a program needn't handle non-finite values.
Results may differ from a plain program's by a relative error of at most 0.0052.
Values may be sent and summed in bfloat16 or wider, within the bound.
No kernel may reach another device: no remote copies, remote signals or barrier semaphores. Data moves between devices by JAX's collectives and lax.ppermute only.
A program may use at most 128 MiB of HBM per device.

v0:
```python
import jax
import jax.numpy as jnp
from jax import lax
from jax.sharding import PartitionSpec as P

C = 320
GROUPS = 32
EPSILON = 1e-06


def with_halo(block, sides, width):
    for axis, dim in sides:
        count = lax.axis_size(axis)
        forward = [(i, i + 1) for i in range(count - 1)]
        backward = [(target, source) for source, target in forward]
        low = lax.ppermute(
            lax.slice_in_dim(block, block.shape[dim] - width, None, axis=dim), axis, forward
        )
        high = lax.ppermute(lax.slice_in_dim(block, 0, width, axis=dim), axis, backward)
        block = jnp.concatenate([low, block, high], axis=dim)
    return block


def spatial_taps(running, channel_slab, weight_piece, rows, width):
    for row_tap in range(3):
        for col_tap in range(3):
            window = channel_slab[:, row_tap : row_tap + rows, :, col_tap : col_tap + width]
            running = running + jnp.einsum(
                "frcw,co->frow",
                window,
                weight_piece[row_tap, col_tap],
                preferred_element_type=jnp.float32,
            )
    return running


def temporal_taps(running, channel_slab, weight_piece, frames):
    for frame_tap in range(3):
        window = channel_slab[frame_tap : frame_tap + frames]
        running = running + jnp.einsum(
            "frcw,co->frow", window, weight_piece[frame_tap], preferred_element_type=jnp.float32
        )
    return running


def body(
    video,
    norm1_gain,
    norm1_bias,
    spatial_weight,
    spatial_bias,
    norm2_gain,
    norm2_bias,
    temporal_weight,
    temporal_bias,
):
    frames, rows, local_chan, width = video.shape
    group_size = C // GROUPS
    local_groups = local_chan // group_size
    values = video.astype(jnp.float32)
    grouped = values.reshape(frames, rows, local_groups, group_size, width)
    entries = rows * lax.axis_size("height") * width * group_size
    totals = lax.psum(jnp.sum(grouped, axis=(1, 3, 4)), "height")
    average = (totals / entries).reshape(frames, 1, local_groups, 1, 1)
    centred = grouped - average
    squares = lax.psum(jnp.sum(centred * centred, axis=(1, 3, 4)), "height")
    variance = (squares / entries).reshape(frames, 1, local_groups, 1, 1)
    scaled = (centred * lax.rsqrt(variance + EPSILON)).reshape(frames, rows, local_chan, width)
    act_one = jax.nn.silu(scaled * norm1_gain[:, None] + norm1_bias[:, None]).astype(jnp.bfloat16)
    with_rows = with_halo(act_one, (("height", 1),), 1)
    all_inputs = lax.all_gather(with_rows, "chan", axis=2, tiled=True)
    padded = jnp.pad(all_inputs, ((0, 0), (0, 0), (0, 0), (1, 1)))
    empty = jnp.zeros((frames, rows, local_chan, width), jnp.float32)
    full_spatial = lax.all_gather(spatial_weight, "tm", axis=2, tiled=True)
    spatial_sum = spatial_taps(empty, padded, full_spatial, rows, width)
    hidden = (values + spatial_sum + spatial_bias[:, None]).astype(jnp.bfloat16)
    grouped_two = hidden.astype(jnp.float32).reshape(frames, rows, local_groups, group_size, width)
    entries_two = frames * lax.axis_size("tm") * entries
    totals_two = lax.psum(jnp.sum(grouped_two, axis=(0, 1, 3, 4)), ("tm", "height"))
    average_two = (totals_two / entries_two).reshape(1, 1, local_groups, 1, 1)
    centred_two = grouped_two - average_two
    squares_two = lax.psum(jnp.sum(centred_two * centred_two, axis=(0, 1, 3, 4)), ("tm", "height"))
    variance_two = (squares_two / entries_two).reshape(1, 1, local_groups, 1, 1)
    scaled_two = (centred_two * lax.rsqrt(variance_two + EPSILON)).reshape(
        frames, rows, local_chan, width
    )
    act_two = jax.nn.silu(scaled_two * norm2_gain[:, None] + norm2_bias[:, None]).astype(
        jnp.bfloat16
    )
    wide_two = lax.all_gather(act_two, "chan", axis=2, tiled=True)
    with_frames = with_halo(wide_two, (("tm", 0),), 1)
    full_temporal = lax.all_gather(temporal_weight, "tm", axis=1, tiled=True)
    temporal_sum = temporal_taps(empty, with_frames, full_temporal, frames)
    return (hidden.astype(jnp.float32) + temporal_sum + temporal_bias[:, None]).astype(jnp.bfloat16)


def solution(mesh):
    return jax.shard_map(
        body,
        mesh=mesh,
        in_specs=(
            P(("groups", "tm"), "height", "chan", None),
            P("chan"),
            P("chan"),
            P(None, None, "tm", "chan"),
            P("chan"),
            P("chan"),
            P("chan"),
            P(None, "tm", "chan"),
            P("chan"),
        ),
        out_specs=P(("groups", "tm"), "height", "chan", None),
        check_vma=False,
    )
```

profile of v0, /device:TPU:0, one launch (start us, length us, event | category | flops | bytes accessed | tf_op | source)
XLA Modules:
  0.0 309.7 jit_solution(8180734178120804956)
XLA Ops:
  9.2 5.8 %psum.28 = f32[2,16]{1,0:T(2,128)S(1)} all-reduce(f32[2,16]{1,0:T(2,128)S(1)} %reduce_sum.51), channel_id=1, replica_groups=mesh['groups'=2,'tm'=4,'height'=2,'chan'=2] {'height'}, use_global_device_ids=true, to_apply=%region_2.0 | all-reduce | flops 32 | bytes 256 | tf_op jit(solution)/shard_map/psum | solution.py:63
  18.1 4.9 %psum.29 = f32[2,16]{1,0:T(2,128)S(1)} all-reduce(f32[2,16]{1,0:T(2,128)S(1)} %reduce_sum.54), channel_id=1, replica_groups=mesh['groups'=2,'tm'=4,'height'=2,'chan'=2] {'height'}, use_global_device_ids=true, to_apply=%region_5.6 | all-reduce | flops 32 | bytes 256 | tf_op jit(solution)/shard_map/psum | solution.py:66
  25.6 4.1 %collective-permute-start = (bf16[2,1,160,128]{3,2,1,0:T(8,128)(2,1)S(1)}, bf16[2,1,160,128]{3,2,1,0:T(8,128)(2,1)S(1)}, u32[]{:S(2)}, u32[]{:S(2)}) collective-permute-start(bf16[2,1,160,128]{3,2,1,0:T(8,128)(2,1)S(1)} %get-tuple-element.7), channel_id=1, source_target_pairs={{0,2},{1,3},{4,6},{5,7},{8,10},{9,11},{12,14},{13,15},{16,18},{17,... | collective-permute-start | bytes 245768 | tf_op jit(solution)/shard_map/ppermute | solution.py:16
  31.7 4.3 %collective-permute-done.1 = bf16[2,1,160,128]{3,2,1,0:T(8,128)(2,1)S(1)} collective-permute-done((bf16[2,1,160,128]{3,2,1,0:T(8,128)(2,1)S(1)}, bf16[2,1,160,128]{3,2,1,0:T(8,128)(2,1)S(1)}, u32[]{:S(2)}, u32[]{:S(2)}) %collective-permute-start.1) | collective-permute-done | bytes 81952 | tf_op jit(solution)/shard_map/ppermute | solution.py:19
  38.5 33.1 %all_gather.13 = bf16[3,3,320,160]{3,1,0,2:T(4,128)(2,1)S(1)} all-gather(bf16[3,3,80,160]{3,1,0,2:T(4,128)(2,1)S(1)} %copy.28), channel_id=1, replica_groups=mesh['groups'=2,'tm'=4,'height'=2,'chan'=2] {'tm'}, dimensions={2}, use_global_device_ids=true | all-gather | bytes 1152000 | tf_op jit(solution)/shard_map/all_gather | solution.py:74
  77.8 4.6 %fusion.26 = f32[2,36,128,160]{2,3,1,0:T(8,128)S(1)} fusion(bf16[2,38,320,128]{3,2,1,0:T(8,128)(2,1)} %all-gather.3.cloned.1.call-done, bf16[1,1,320,160]{2,3,1,0:T(8,128)(2,1)S(1)} %copy.54), kind=kOutput, calls=%fused_computation.38 | convolution fusion | flops 943718400 | bytes 12226560 | tf_op jit(solution)/shard_map/frcw,co->frow/dot_general | solution.py:28
  82.5 4.3 %fusion.27 = f32[2,36,128,160]{2,3,1,0:T(8,128)} fusion(bf16[2,38,320,128]{3,2,1,0:T(8,128)(2,1)S(1)} %copy-done, bf16[1,1,320,160]{2,3,1,0:T(8,128)(2,1)S(1)} %copy.56), kind=kOutput, calls=%fused_computation.39 | convolution fusion | flops 943718400 | bytes 12226560 | tf_op jit(solution)/shard_map/frcw,co->frow/dot_general | solution.py:28
  86.8 4.4 %fusion.28 = f32[2,36,128,160]{2,3,1,0:T(8,128)} fusion(bf16[2,38,320,128]{3,2,1,0:T(8,128)(2,1)S(1)} %copy-done, bf16[1,1,320,160]{2,3,1,0:T(8,128)(2,1)S(1)} %copy.57), kind=kOutput, calls=%fused_computation.40 | convolution fusion | flops 943718400 | bytes 12226560 | tf_op jit(solution)/shard_map/frcw,co->frow/dot_general | solution.py:28
  91.2 4.3 %fusion.29 = f32[2,36,128,160]{2,3,1,0:T(8,128)} fusion(bf16[2,38,320,128]{3,2,1,0:T(8,128)(2,1)S(1)} %copy-done, bf16[1,1,320,160]{2,3,1,0:T(8,128)(2,1)S(1)} %copy.59), kind=kOutput, calls=%fused_computation.41 | convolution fusion | flops 943718400 | bytes 12226560 | tf_op jit(solution)/shard_map/frcw,co->frow/dot_general | solution.py:28
  95.5 4.4 %fusion.30 = f32[2,36,128,160]{2,3,1,0:T(8,128)} fusion(bf16[2,38,320,128]{3,2,1,0:T(8,128)(2,1)S(1)} %copy-done, bf16[1,1,320,160]{2,3,1,0:T(8,128)(2,1)S(1)} %copy.60), kind=kOutput, calls=%fused_computation.42 | convolution fusion | flops 943718400 | bytes 12226560 | tf_op jit(solution)/shard_map/frcw,co->frow/dot_general | solution.py:28
  100.0 4.2 %fusion.36 = f32[2,36,128,160]{2,3,1,0:T(8,128)} fusion(bf16[2,38,320,128]{3,2,1,0:T(8,128)(2,1)S(1)} %copy-done, bf16[1,1,320,160]{2,3,1,0:T(8,128)(2,1)S(1)} %copy-done.3), kind=kOutput, calls=%fused_computation.50 | convolution fusion | flops 943718400 | bytes 11919360 | tf_op jit(solution)/shard_map/frcw,co->frow/dot_general | solution.py:28
  104.2 4.4 %fusion.38 = f32[2,36,128,160]{2,3,1,0:T(8,128)} fusion(bf16[2,38,320,128]{3,2,1,0:T(8,128)(2,1)S(1)} %copy-done, bf16[1,1,320,160]{2,3,1,0:T(8,128)(2,1)S(1)} %copy-done.4), kind=kOutput, calls=%fused_computation.52 | convolution fusion | flops 943718400 | bytes 11919360 | tf_op jit(solution)/shard_map/frcw,co->frow/dot_general | solution.py:28
  108.6 4.2 %fusion.40 = f32[2,36,128,160]{2,3,1,0:T(8,128)} fusion(bf16[2,38,320,128]{3,2,1,0:T(8,128)(2,1)S(1)} %copy-done, bf16[1,1,320,160]{2,3,1,0:T(8,128)(2,1)S(1)} %copy-done.5), kind=kOutput, calls=%fused_computation.54 | convolution fusion | flops 943718400 | bytes 11919360 | tf_op jit(solution)/shard_map/frcw,co->frow/dot_general | solution.py:28
  112.8 17.5 %convert_reduce_fusion = (f32[160]{0:T(256)S(1)}, bf16[2,36,160,128]{3,2,1,0:T(8,128)(2,1)}) fusion(f32[160]{0:T(256)S(1)} %copy-done.8, bf16[2,38,320,128]{3,2,1,0:T(8,128)(2,1)S(1)} %copy-done, bf16[1,1,320,160]{2,3,1,0:T(8,128)(2,1)S(1)} %copy.62, f32[2,36,128,160]{2,3,1,0:T(8,128)} %fusion.36, f32[2,36,128,160]{2,3,1,0:T(8,128)} %fusion.30, ...), kind=kOutput, calls=%fused_computation.8 | convolution fusion | flops 964362112 | bytes 59413760 | tf_op jit(solution)/shard_map/frcw,co->frow/dot_general | solution.py:28
  130.5 19.8 %psum.30 = f32[16]{0:T(128)S(1)} all-reduce(f32[16]{0:T(128)S(1)} %reduce_sum.72), channel_id=1, replica_groups=mesh['groups'=2,'tm'=4,'height'=2,'chan'=2] {'tm','height'}, use_global_device_ids=true, to_apply=%region_8.9 | all-reduce | flops 16 | bytes 128 | tf_op jit(solution)/shard_map/psum | solution.py:79
  153.4 17.1 %psum.31 = f32[16]{0:T(128)S(1)} all-reduce(f32[16]{0:T(128)S(1)} %reduce_sum.75), channel_id=1, replica_groups=mesh['groups'=2,'tm'=4,'height'=2,'chan'=2] {'tm','height'}, use_global_device_ids=true, to_apply=%region_11.12 | all-reduce | flops 16 | bytes 128 | tf_op jit(solution)/shard_map/psum | solution.py:82
  170.8 5.1 %fusion.12 = bf16[2,36,160,128]{3,2,1,0:T(8,128)(2,1)} fusion(bf16[2,36,160,128]{3,2,1,0:T(8,128)(2,1)} %get-tuple-element.22, f32[160]{0:T(256)S(1)} %copy-done.12, f32[160]{0:T(256)S(1)} %copy-done.13, f32[160]{0:T(256)S(1)} %mul.67, f32[160]{0:T(256)S(1)} %sub.33), kind=kLoop, calls=%fused_computation.24 | loop fusion | flops 14745600 | bytes 5900800 | tf_op jit(solution)/shard_map/convert_element_type | solution.py:87
  175.9 15.1 %all-gather.5.cloned.1.call-done = bf16[2,36,320,128]{3,2,1,0:T(8,128)(2,1)} async-done(((bf16[2,36,160,128]{3,2,1,0:T(8,128)(2,1)}), bf16[2,36,320,128]{3,2,1,0:T(8,128)(2,1)}) %all-gather.5.cloned.1.call-update) | async-done | bytes 5898256 | tf_op jit(solution)/shard_map/all_gather | solution.py:90
  190.9 5.6 %fusion.65 = (bf16[1,36,320,128]{3,2,1,0:T(8,128)(2,1)}, bf16[1,36,320,128]{3,2,1,0:T(8,128)(2,1)}) fusion(bf16[2,36,320,128]{3,2,1,0:T(8,128)(2,1)} %all-gather.5.cloned.1.call-done), kind=kLoop, calls=%fused_computation.82 | loop fusion | bytes 11796480 | tf_op jit(solution)/shard_map/slice | solution.py:19
  196.5 5.3 %collective-permute-start.2 = (bf16[1,36,320,128]{3,2,1,0:T(8,128)(2,1)}, bf16[1,36,320,128]{3,2,1,0:T(8,128)(2,1)}, u32[]{:S(2)}, u32[]{:S(2)}) collective-permute-start(bf16[1,36,320,128]{3,2,1,0:T(8,128)(2,1)} %get-tuple-element.6), channel_id=1, source_target_pairs={{0,4},{4,8},{8,12},{1,5},{5,9},{9,13},{2,6},{6,10},{10,14},{3,7},{... | collective-permute-start | bytes 8847368 | tf_op jit(solution)/shard_map/ppermute | solution.py:16
  203.2 79.8 %all_gather.15 = bf16[3,320,160]{2,0,1:T(4,128)(2,1)S(1)} all-gather(bf16[3,80,160]{2,0,1:T(4,128)(2,1)S(1)} %copy.38), channel_id=1, replica_groups=mesh['groups'=2,'tm'=4,'height'=2,'chan'=2] {'tm'}, dimensions={1}, use_global_device_ids=true | all-gather | bytes 384000 | tf_op jit(solution)/shard_map/all_gather | solution.py:92
  284.3 4.5 %fusion.45 = f32[2,36,128,160]{2,3,1,0:T(8,128)S(1)} fusion(bf16[2,36,320,128]{3,2,1,0:T(8,128)(2,1)} %all-gather.5.cloned.1.call-done, bf16[1,320,160]{1,2,0:T(8,128)(2,1)S(1)} %copy.64), kind=kOutput, calls=%fused_computation.58 | convolution fusion | flops 943718400 | bytes 11898880 | tf_op jit(solution)/shard_map/frcw,co->frow/dot_general | solution.py:40
  288.9 6.2 %fusion.34 = f32[2,36,128,160]{2,3,1,0:T(8,128)} fusion(bf16[2,36,320,128]{3,2,1,0:T(8,128)(2,1)S(1)} %bitcast.94, bf16[1,36,320,128]{3,2,1,0:T(8,128)(2,1)} %collective-permute-done.2, bf16[1,320,160]{1,2,0:T(8,128)(2,1)S(1)} %copy.63), kind=kOutput, calls=%fused_computation.48 | convolution fusion | flops 955514880 | bytes 14848000 | tf_op jit(solution)/shard_map/frcw,co->frow/dot_general | solution.py:40
  295.1 7.7 %fusion.25 = bf16[2,36,160,128]{3,2,1,0:T(8,128)(2,1)} fusion(bf16[2,36,160,128]{3,2,1,0:T(8,128)(2,1)S(1)} %copy-done.1, f32[2,36,128,160]{2,3,1,0:T(8,128)} %fusion.34, f32[2,36,128,160]{2,3,1,0:T(8,128)S(1)} %fusion.45, f32[160]{0:T(256)S(1)} %copy-done.9, bf16[1,36,320,128]{3,2,1,0:T(8,128)(2,1)} %collective-permute-done.3, ...), kind=kOutput, calls=%fused_computation.37 | convolution fusion | flops 964362240 | bytes 26645120 | tf_op jit(solution)/shard_map/frcw,co->frow/dot_general | solution.py:40
  (85 shorter events, 25.1 us)
Async XLA Ops:
  6.5 16.7 %copy-start.2 = (bf16[2,36,160,128]{3,2,1,0:T(8,128)(2,1)S(1)}, bf16[2,36,160,128]{3,2,1,0:T(8,128)(2,1)}, u32[]{:S(2)}) copy-start(bf16[2,36,160,128]{3,2,1,0:T(8,128)(2,1)} %param.9) | copy-start | bytes 8847364
  6.5 16.7 %copy-start.11 = (f32[160]{0:T(256)S(1)}, f32[160]{0:T(256)}, u32[]{:S(2)}) copy-start(f32[160]{0:T(256)} %param.10) | copy-start | bytes 1924
  6.5 16.7 %copy-start.10 = (f32[160]{0:T(256)S(1)}, f32[160]{0:T(256)}, u32[]{:S(2)}) copy-start(f32[160]{0:T(256)} %param.11) | copy-start | bytes 1924
  6.5 71.3 %all-gather.3.cloned.1.call-start = ((), (), s32[]{:S(2)}) async-start(), calls=%async_computation | async-start | bytes 9338880 | tf_op jit(solution)/shard_map/all_gather | solution.py:71
  25.6 12.6 %copy-start.6 = (bf16[3,3,80,160]{3,2,1,0:T(8,128)(2,1)S(1)}, bf16[3,3,80,160]{3,2,1,0:T(8,128)(2,1)}, u32[]{:S(2)}) copy-start(bf16[3,3,80,160]{3,2,1,0:T(8,128)(2,1)} %param.12) | copy-start | bytes 691204
  25.6 6.1 %collective-permute-start = (bf16[2,1,160,128]{3,2,1,0:T(8,128)(2,1)S(1)}, bf16[2,1,160,128]{3,2,1,0:T(8,128)(2,1)S(1)}, u32[]{:S(2)}, u32[]{:S(2)}) collective-permute-start(bf16[2,1,160,128]{3,2,1,0:T(8,128)(2,1)S(1)} %get-tuple-element.7), channel_id=1, source_target_pairs={{0,2},{1,3},{4,6},{5,7},{8,10},{9,11},{12,14},{13,15},{16,18},{17,... | collective-permute-start | bytes 245768 | tf_op jit(solution)/shard_map/ppermute | solution.py:16
  29.7 6.3 %collective-permute-start.1 = (bf16[2,1,160,128]{3,2,1,0:T(8,128)(2,1)S(1)}, bf16[2,1,160,128]{3,2,1,0:T(8,128)(2,1)S(1)}, u32[]{:S(2)}, u32[]{:S(2)}) collective-permute-start(bf16[2,1,160,128]{3,2,1,0:T(8,128)(2,1)S(1)} %get-tuple-element.8), channel_id=1, source_target_pairs={{2,0},{3,1},{6,4},{7,5},{10,8},{11,9},{14,12},{15,13},{18,16},{19,... | collective-permute-start | bytes 245768 | tf_op jit(solution)/shard_map/ppermute | solution.py:19
  38.1 152.8 %all-gather.5.cloned.1.call-start = ((), (), s32[]{:S(2)}) async-start(), calls=%async_computation.1 | async-start | bytes 8847360 | tf_op jit(solution)/shard_map/all_gather | solution.py:90
  77.8 4.7 %copy-start = (bf16[2,38,320,128]{3,2,1,0:T(8,128)(2,1)S(1)}, bf16[2,38,320,128]{3,2,1,0:T(8,128)(2,1)}, u32[]{:S(2)}) copy-start(bf16[2,38,320,128]{3,2,1,0:T(8,128)(2,1)} %all-gather.3.cloned.1.call-done) | copy-start | bytes 18677764
  95.5 4.4 %copy-start.3 = (bf16[1,1,320,160]{2,3,1,0:T(8,128)(2,1)S(1)}, bf16[1,1,320,160]{2,3,1,0:T(8,128)(2,1)}, u32[]{:S(2)}) copy-start(bf16[1,1,320,160]{2,3,1,0:T(8,128)(2,1)} %copy.61) | copy-start | bytes 307204
  100.0 4.2 %copy-start.4 = (bf16[1,1,320,160]{2,3,1,0:T(8,128)(2,1)S(1)}, bf16[1,1,320,160]{2,3,1,0:T(8,128)(2,1)}, u32[]{:S(2)}) copy-start(bf16[1,1,320,160]{2,3,1,0:T(8,128)(2,1)} %copy.58) | copy-start | bytes 307204
  104.2 4.4 %copy-start.5 = (bf16[1,1,320,160]{2,3,1,0:T(8,128)(2,1)S(1)}, bf16[1,1,320,160]{2,3,1,0:T(8,128)(2,1)}, u32[]{:S(2)}) copy-start(bf16[1,1,320,160]{2,3,1,0:T(8,128)(2,1)} %copy.55) | copy-start | bytes 307204
  108.6 4.2 %copy-start.8 = (f32[160]{0:T(256)S(1)}, f32[160]{0:T(256)}, u32[]{:S(2)}) copy-start(f32[160]{0:T(256)} %param.13) | copy-start | bytes 1924
  112.8 57.9 %copy-start.12 = (f32[160]{0:T(256)S(1)}, f32[160]{0:T(256)}, u32[]{:S(2)}) copy-start(f32[160]{0:T(256)} %param.15) | copy-start | bytes 1924
  112.8 58.0 %copy-start.13 = (f32[160]{0:T(256)S(1)}, f32[160]{0:T(256)}, u32[]{:S(2)}) copy-start(f32[160]{0:T(256)} %param.14) | copy-start | bytes 1924
  175.9 27.3 %copy-start.7 = (bf16[3,80,160]{2,1,0:T(8,128)(2,1)S(1)}, bf16[3,80,160]{2,1,0:T(8,128)(2,1)}, u32[]{:S(2)}) copy-start(bf16[3,80,160]{2,1,0:T(8,128)(2,1)} %param.16) | copy-start | bytes 230404
  196.5 92.3 %collective-permute-start.2 = (bf16[1,36,320,128]{3,2,1,0:T(8,128)(2,1)}, bf16[1,36,320,128]{3,2,1,0:T(8,128)(2,1)}, u32[]{:S(2)}, u32[]{:S(2)}) collective-permute-start(bf16[1,36,320,128]{3,2,1,0:T(8,128)(2,1)} %get-tuple-element.6), channel_id=1, source_target_pairs={{0,4},{4,8},{8,12},{1,5},{5,9},{9,13},{2,6},{6,10},{10,14},{3,7},{... | collective-permute-start | bytes 8847368 | tf_op jit(solution)/shard_map/ppermute | solution.py:16
  201.9 93.3 %collective-permute-start.3 = (bf16[1,36,320,128]{3,2,1,0:T(8,128)(2,1)}, bf16[1,36,320,128]{3,2,1,0:T(8,128)(2,1)}, u32[]{:S(2)}, u32[]{:S(2)}) collective-permute-start(bf16[1,36,320,128]{3,2,1,0:T(8,128)(2,1)} %get-tuple-element.5), channel_id=1, source_target_pairs={{4,0},{8,4},{12,8},{5,1},{9,5},{13,9},{6,2},{10,6},{14,10},{7,3},{... | collective-permute-start | bytes 8847368 | tf_op jit(solution)/shard_map/ppermute | solution.py:19
  284.1 4.8 %slice-start = ((s8[5898240]{0:T(1024)(128)(4,1)}), s8[1703936]{0:T(1024)(128)(4,1)S(1)}, s32[]{:S(2)}) async-start(s8[5898240]{0:T(1024)(128)(4,1)} %bitcast.93), calls=%async_computation.2 | async-start | bytes 3407872
  284.3 4.6 %slice-start.1 = ((s8[5898240]{0:T(1024)(128)(4,1)}), s8[4194304]{0:T(1024)(128)(4,1)S(1)}, s32[]{:S(2)}) async-start(s8[5898240]{0:T(1024)(128)(4,1)} %bitcast.93), calls=%async_computation.3 | async-start | bytes 8388608
  288.8 6.3 %copy-start.1 = (bf16[2,36,160,128]{3,2,1,0:T(8,128)(2,1)S(1)}, bf16[2,36,160,128]{3,2,1,0:T(8,128)(2,1)}, u32[]{:S(2)}) copy-start(bf16[2,36,160,128]{3,2,1,0:T(8,128)(2,1)} %get-tuple-element.22) | copy-start | bytes 8847364
  288.9 6.3 %copy-start.9 = (f32[160]{0:T(256)S(1)}, f32[160]{0:T(256)}, u32[]{:S(2)}) copy-start(f32[160]{0:T(256)} %param.17) | copy-start | bytes 1924
Sparse Core Ops, SparseCore 0:
  38.3 16.9 all-gather.2
  176.0 14.9 all-gather.4
where the time goes:
time: 310 us
  blocking collectives  161 us (52%)
  matrix products  70.9 us (23%)
  waiting for transfers between devices  20.2 us (7%)
  other arithmetic  17.9 us (6%)
  local copies, waits for them, and re-layouts  14.5 us (5%)
  between operations  13.7 us (4%)
  starting transfers between devices  12 us (4%)
    all_gather x1, blocking collectives, body(): full_temporal = lax.all_gather(temporal_weight, 'tm', axis=1, tiled=True)  79.8 us
    dot_general x9, matrix products, spatial_taps(): jnp.einsum('frcw,co->frow', window, weight_piece[row_tap, col_tap], prefe...  52.5 us
    all_gather x1, blocking collectives, body(): full_spatial = lax.all_gather(spatial_weight, 'tm', axis=2, tiled=True)  33.1 us
    psum x1, blocking collectives, body(): lax.psum(jnp.sum(grouped_two, axis=(0, 1, 3, 4)), ('tm', 'height'))  19.8 us
    dot_general x3, matrix products, temporal_taps(): jnp.einsum('frcw,co->frow', window, weight_piece[frame_tap], preferred_el...  18.4 us
    psum x1, blocking collectives, body(): lax.psum(jnp.sum(centred_two * centred_two, axis=(0, 1, 3, 4)), ('tm', 'h...  17.1 us
    all_gather x1, waiting for transfers between devices, body(): wide_two = lax.all_gather(act_two, 'chan', axis=2, tiled=True)  15.1 us
    ppermute x2, starting transfers between devices, with_halo(): lax.ppermute(lax.slice_in_dim(block, block.shape[dim] - width, None, axis...  9.4 us
  transfers between devices with their start and end apart: 6, of which 3 were waited for; matrix products, arithmetic and copies ran while one was open for 6% of the time, Pallas kernels for 0%

commit v1 on v0

--- a/solution.py
+++ b/solution.py
@@ -79,7 +79,9 @@
     totals_two = lax.psum(jnp.sum(grouped_two, axis=(0, 1, 3, 4)), ("tm", "height"))
     average_two = (totals_two / entries_two).reshape(1, 1, local_groups, 1, 1)
     centred_two = grouped_two - average_two
-    squares_two = lax.psum(jnp.sum(centred_two * centred_two, axis=(0, 1, 3, 4)), ("tm", "height"))
+    block_2 = jnp.sum(centred_two * centred_two, axis=(0, 1, 3, 4))
+    blocks = lax.all_gather(block_2, ("tm", "height"), axis=0, tiled=False)
+    squares_two = blocks.sum(axis=0)
     variance_two = (squares_two / entries_two).reshape(1, 1, local_groups, 1, 1)
     scaled_two = (centred_two * lax.rsqrt(variance_two + EPSILON)).reshape(
         frames, rows, local_chan, width

time: 310 us -> 312 us (level)
    psum x1 -> x0, blocking collectives: 17.1 us -> none  [body(): lax.psum(jnp.sum(centred_two * centred_two, axis=(0, 1, 3, 4)), ('tm', 'h...]
    unnamed x0 -> x1, blocking collectives: none -> 17.1 us
where the time goes in v1:
time: 312 us; the launch traced here: 311 us
  blocking collectives  160 us (51%)
  matrix products  70.9 us (23%)
  waiting for transfers between devices  20.1 us (6%)
  other arithmetic  17.9 us (6%)
  local copies, waits for them, and re-layouts  15.5 us (5%)
  between operations  14.4 us (5%)
  starting transfers between devices  12 us (4%)
    all_gather x1, blocking collectives, body(): full_temporal = lax.all_gather(temporal_weight, 'tm', axis=1, tiled=True)  79.8 us
    dot_general x9, matrix products, spatial_taps(): jnp.einsum('frcw,co->frow', window, weight_piece[row_tap, col_tap], prefe...  52.4 us
    all_gather x1, blocking collectives, body(): full_spatial = lax.all_gather(spatial_weight, 'tm', axis=2, tiled=True)  33.1 us
    psum x1, blocking collectives, body(): lax.psum(jnp.sum(grouped_two, axis=(0, 1, 3, 4)), ('tm', 'height'))  19.8 us
    dot_general x3, matrix products, temporal_taps(): jnp.einsum('frcw,co->frow', window, weight_piece[frame_tap], preferred_el...  18.4 us
    unnamed x1, blocking collectives  17.1 us
    all_gather x1, waiting for transfers between devices, body(): wide_two = lax.all_gather(act_two, 'chan', axis=2, tiled=True)  15.1 us
    ppermute x2, starting transfers between devices, with_halo(): lax.ppermute(lax.slice_in_dim(block, block.shape[dim] - width, None, axis...  9.4 us
  transfers between devices with their start and end apart: 6, of which 3 were waited for; matrix products, arithmetic and copies ran while one was open for 6% of the time, Pallas kernels for 0%

profile of v1, /device:TPU:0, one launch (start us, length us, event | category | flops | bytes accessed | tf_op | source)
XLA Modules:
  0.0 311.4 jit_solution(11176957732759495957)
XLA Ops:
  9.2 5.8 %psum.21 = f32[2,16]{1,0:T(2,128)S(1)} all-reduce(f32[2,16]{1,0:T(2,128)S(1)} %reduce_sum.59), channel_id=1, replica_groups=mesh['groups'=2,'tm'=4,'height'=2,'chan'=2] {'height'}, use_global_device_ids=true, to_apply=%region_2.0 | all-reduce | flops 32 | bytes 256 | tf_op jit(solution)/shard_map/psum | solution.py:63
  18.1 4.9 %psum.22 = f32[2,16]{1,0:T(2,128)S(1)} all-reduce(f32[2,16]{1,0:T(2,128)S(1)} %reduce_sum.62), channel_id=1, replica_groups=mesh['groups'=2,'tm'=4,'height'=2,'chan'=2] {'height'}, use_global_device_ids=true, to_apply=%region_5.6 | all-reduce | flops 32 | bytes 256 | tf_op jit(solution)/shard_map/psum | solution.py:66
  25.6 4.1 %collective-permute-start = (bf16[2,1,160,128]{3,2,1,0:T(8,128)(2,1)S(1)}, bf16[2,1,160,128]{3,2,1,0:T(8,128)(2,1)S(1)}, u32[]{:S(2)}, u32[]{:S(2)}) collective-permute-start(bf16[2,1,160,128]{3,2,1,0:T(8,128)(2,1)S(1)} %get-tuple-element.7), channel_id=1, source_target_pairs={{0,2},{1,3},{4,6},{5,7},{8,10},{9,11},{12,14},{13,15},{16,18},{17,... | collective-permute-start | bytes 245768 | tf_op jit(solution)/shard_map/ppermute | solution.py:16
  31.7 4.3 %collective-permute-done.1 = bf16[2,1,160,128]{3,2,1,0:T(8,128)(2,1)S(1)} collective-permute-done((bf16[2,1,160,128]{3,2,1,0:T(8,128)(2,1)S(1)}, bf16[2,1,160,128]{3,2,1,0:T(8,128)(2,1)S(1)}, u32[]{:S(2)}, u32[]{:S(2)}) %collective-permute-start.1) | collective-permute-done | bytes 81952 | tf_op jit(solution)/shard_map/ppermute | solution.py:19
  38.5 33.1 %all_gather.19 = bf16[3,3,320,160]{3,1,0,2:T(4,128)(2,1)S(1)} all-gather(bf16[3,3,80,160]{3,1,0,2:T(4,128)(2,1)S(1)} %copy.28), channel_id=1, replica_groups=mesh['groups'=2,'tm'=4,'height'=2,'chan'=2] {'tm'}, dimensions={2}, use_global_device_ids=true | all-gather | bytes 1152000 | tf_op jit(solution)/shard_map/all_gather | solution.py:74
  78.5 4.6 %fusion.26 = f32[2,36,128,160]{2,3,1,0:T(8,128)S(1)} fusion(bf16[2,38,320,128]{3,2,1,0:T(8,128)(2,1)} %all-gather.4.cloned.1.call-done, bf16[1,1,320,160]{2,3,1,0:T(8,128)(2,1)S(1)} %copy.54), kind=kOutput, calls=%fused_computation.38 | convolution fusion | flops 943718400 | bytes 12226560 | tf_op jit(solution)/shard_map/frcw,co->frow/dot_general | solution.py:28
  83.1 4.3 %fusion.27 = f32[2,36,128,160]{2,3,1,0:T(8,128)} fusion(bf16[2,38,320,128]{3,2,1,0:T(8,128)(2,1)S(1)} %copy-done, bf16[1,1,320,160]{2,3,1,0:T(8,128)(2,1)S(1)} %copy.56), kind=kOutput, calls=%fused_computation.39 | convolution fusion | flops 943718400 | bytes 12226560 | tf_op jit(solution)/shard_map/frcw,co->frow/dot_general | solution.py:28
  87.5 4.4 %fusion.28 = f32[2,36,128,160]{2,3,1,0:T(8,128)} fusion(bf16[2,38,320,128]{3,2,1,0:T(8,128)(2,1)S(1)} %copy-done, bf16[1,1,320,160]{2,3,1,0:T(8,128)(2,1)S(1)} %copy.57), kind=kOutput, calls=%fused_computation.40 | convolution fusion | flops 943718400 | bytes 12226560 | tf_op jit(solution)/shard_map/frcw,co->frow/dot_general | solution.py:28
  91.8 4.3 %fusion.29 = f32[2,36,128,160]{2,3,1,0:T(8,128)} fusion(bf16[2,38,320,128]{3,2,1,0:T(8,128)(2,1)S(1)} %copy-done, bf16[1,1,320,160]{2,3,1,0:T(8,128)(2,1)S(1)} %copy.59), kind=kOutput, calls=%fused_computation.41 | convolution fusion | flops 943718400 | bytes 12226560 | tf_op jit(solution)/shard_map/frcw,co->frow/dot_general | solution.py:28
  96.2 4.4 %fusion.30 = f32[2,36,128,160]{2,3,1,0:T(8,128)} fusion(bf16[2,38,320,128]{3,2,1,0:T(8,128)(2,1)S(1)} %copy-done, bf16[1,1,320,160]{2,3,1,0:T(8,128)(2,1)S(1)} %copy.60), kind=kOutput, calls=%fused_computation.42 | convolution fusion | flops 943718400 | bytes 12226560 | tf_op jit(solution)/shard_map/frcw,co->frow/dot_general | solution.py:28
  100.6 4.2 %fusion.36 = f32[2,36,128,160]{2,3,1,0:T(8,128)} fusion(bf16[2,38,320,128]{3,2,1,0:T(8,128)(2,1)S(1)} %copy-done, bf16[1,1,320,160]{2,3,1,0:T(8,128)(2,1)S(1)} %copy-done.3), kind=kOutput, calls=%fused_computation.50 | convolution fusion | flops 943718400 | bytes 11919360 | tf_op jit(solution)/shard_map/frcw,co->frow/dot_general | solution.py:28
  104.8 4.4 %fusion.38 = f32[2,36,128,160]{2,3,1,0:T(8,128)} fusion(bf16[2,38,320,128]{3,2,1,0:T(8,128)(2,1)S(1)} %copy-done, bf16[1,1,320,160]{2,3,1,0:T(8,128)(2,1)S(1)} %copy-done.4), kind=kOutput, calls=%fused_computation.52 | convolution fusion | flops 943718400 | bytes 11919360 | tf_op jit(solution)/shard_map/frcw,co->frow/dot_general | solution.py:28
  109.3 4.2 %fusion.40 = f32[2,36,128,160]{2,3,1,0:T(8,128)} fusion(bf16[2,38,320,128]{3,2,1,0:T(8,128)(2,1)S(1)} %copy-done, bf16[1,1,320,160]{2,3,1,0:T(8,128)(2,1)S(1)} %copy-done.5), kind=kOutput, calls=%fused_computation.54 | convolution fusion | flops 943718400 | bytes 11919360 | tf_op jit(solution)/shard_map/frcw,co->frow/dot_general | solution.py:28
  113.5 17.5 %convert_reduce_fusion = (f32[160]{0:T(256)S(1)}, bf16[2,36,160,128]{3,2,1,0:T(8,128)(2,1)}) fusion(f32[160]{0:T(256)S(1)} %copy-done.8, bf16[2,38,320,128]{3,2,1,0:T(8,128)(2,1)S(1)} %copy-done, bf16[1,1,320,160]{2,3,1,0:T(8,128)(2,1)S(1)} %copy.62, f32[2,36,128,160]{2,3,1,0:T(8,128)} %fusion.36, f32[2,36,128,160]{2,3,1,0:T(8,128)} %fusion.30, ...), kind=kOutput, calls=%fused_computation.8 | convolution fusion | flops 964362112 | bytes 59413760 | tf_op jit(solution)/shard_map/frcw,co->frow/dot_general | solution.py:28
  131.9 19.8 %psum.23 = f32[16]{0:T(128)S(1)} all-reduce(f32[16]{0:T(128)S(1)} %reduce_sum.81), channel_id=1, replica_groups=mesh['groups'=2,'tm'=4,'height'=2,'chan'=2] {'tm','height'}, use_global_device_ids=true, to_apply=%region_8.9 | all-reduce | flops 16 | bytes 128 | tf_op jit(solution)/shard_map/psum | solution.py:79
  155.1 17.1 %all-reduce.1 = f32[128]{0:T(128)S(1)} all-reduce(f32[128]{0:T(128)S(1)} %dynamic-update-slice), channel_id=2, replica_groups=mesh['groups'=2,'tm'=4,'height'=2,'chan'=2] {'tm','height'}, use_global_device_ids=true, to_apply=%add.1 | all-reduce | flops 128 | bytes 1024
  172.5 5.1 %fusion.12 = bf16[2,36,160,128]{3,2,1,0:T(8,128)(2,1)} fusion(bf16[2,36,160,128]{3,2,1,0:T(8,128)(2,1)} %get-tuple-element.22, f32[160]{0:T(256)S(1)} %copy-done.12, f32[160]{0:T(256)S(1)} %copy-done.13, f32[160]{0:T(256)S(1)} %mul.67, f32[160]{0:T(256)S(1)} %sub.33), kind=kLoop, calls=%fused_computation.24 | loop fusion | flops 14745600 | bytes 5900800 | tf_op jit(solution)/shard_map/convert_element_type | solution.py:89
  177.6 15.1 %all-gather.6.cloned.1.call-done = bf16[2,36,320,128]{3,2,1,0:T(8,128)(2,1)} async-done(((bf16[2,36,160,128]{3,2,1,0:T(8,128)(2,1)}), bf16[2,36,320,128]{3,2,1,0:T(8,128)(2,1)}) %all-gather.6.cloned.1.call-update) | async-done | bytes 5898256 | tf_op jit(solution)/shard_map/all_gather | solution.py:92
  192.6 5.6 %fusion.65 = (bf16[1,36,320,128]{3,2,1,0:T(8,128)(2,1)}, bf16[1,36,320,128]{3,2,1,0:T(8,128)(2,1)}) fusion(bf16[2,36,320,128]{3,2,1,0:T(8,128)(2,1)} %all-gather.6.cloned.1.call-done), kind=kLoop, calls=%fused_computation.82 | loop fusion | bytes 11796480 | tf_op jit(solution)/shard_map/slice | solution.py:19
  198.2 5.3 %collective-permute-start.2 = (bf16[1,36,320,128]{3,2,1,0:T(8,128)(2,1)}, bf16[1,36,320,128]{3,2,1,0:T(8,128)(2,1)}, u32[]{:S(2)}, u32[]{:S(2)}) collective-permute-start(bf16[1,36,320,128]{3,2,1,0:T(8,128)(2,1)} %get-tuple-element.6), channel_id=1, source_target_pairs={{0,4},{4,8},{8,12},{1,5},{5,9},{9,13},{2,6},{6,10},{10,14},{3,7},{... | collective-permute-start | bytes 8847368 | tf_op jit(solution)/shard_map/ppermute | solution.py:16
  204.9 79.8 %all_gather.23 = bf16[3,320,160]{2,0,1:T(4,128)(2,1)S(1)} all-gather(bf16[3,80,160]{2,0,1:T(4,128)(2,1)S(1)} %copy.38), channel_id=1, replica_groups=mesh['groups'=2,'tm'=4,'height'=2,'chan'=2] {'tm'}, dimensions={1}, use_global_device_ids=true | all-gather | bytes 384000 | tf_op jit(solution)/shard_map/all_gather | solution.py:94
  286.0 4.5 %fusion.45 = f32[2,36,128,160]{2,3,1,0:T(8,128)S(1)} fusion(bf16[2,36,320,128]{3,2,1,0:T(8,128)(2,1)} %all-gather.6.cloned.1.call-done, bf16[1,320,160]{1,2,0:T(8,128)(2,1)S(1)} %copy.64), kind=kOutput, calls=%fused_computation.58 | convolution fusion | flops 943718400 | bytes 11898880 | tf_op jit(solution)/shard_map/frcw,co->frow/dot_general | solution.py:40
  290.6 6.2 %fusion.34 = f32[2,36,128,160]{2,3,1,0:T(8,128)} fusion(bf16[2,36,320,128]{3,2,1,0:T(8,128)(2,1)S(1)} %bitcast.95, bf16[1,36,320,128]{3,2,1,0:T(8,128)(2,1)} %collective-permute-done.2, bf16[1,320,160]{1,2,0:T(8,128)(2,1)S(1)} %copy.63), kind=kOutput, calls=%fused_computation.48 | convolution fusion | flops 955514880 | bytes 14848000 | tf_op jit(solution)/shard_map/frcw,co->frow/dot_general | solution.py:40
  296.8 7.7 %fusion.25 = bf16[2,36,160,128]{3,2,1,0:T(8,128)(2,1)} fusion(bf16[2,36,160,128]{3,2,1,0:T(8,128)(2,1)S(1)} %copy-done.1, f32[2,36,128,160]{2,3,1,0:T(8,128)} %fusion.34, f32[2,36,128,160]{2,3,1,0:T(8,128)S(1)} %fusion.45, f32[160]{0:T(256)S(1)} %copy-done.9, bf16[1,36,320,128]{3,2,1,0:T(8,128)(2,1)} %collective-permute-done.3, ...), kind=kOutput, calls=%fused_computation.37 | convolution fusion | flops 964362240 | bytes 26645120 | tf_op jit(solution)/shard_map/frcw,co->frow/dot_general | solution.py:40
  (92 shorter events, 26.1 us)
Async XLA Ops:
  6.5 16.7 %copy-start.2 = (bf16[2,36,160,128]{3,2,1,0:T(8,128)(2,1)S(1)}, bf16[2,36,160,128]{3,2,1,0:T(8,128)(2,1)}, u32[]{:S(2)}) copy-start(bf16[2,36,160,128]{3,2,1,0:T(8,128)(2,1)} %param.9) | copy-start | bytes 8847364
  6.5 16.7 %copy-start.11 = (f32[160]{0:T(256)S(1)}, f32[160]{0:T(256)}, u32[]{:S(2)}) copy-start(f32[160]{0:T(256)} %param.10) | copy-start | bytes 1924
  6.5 16.7 %copy-start.10 = (f32[160]{0:T(256)S(1)}, f32[160]{0:T(256)}, u32[]{:S(2)}) copy-start(f32[160]{0:T(256)} %param.11) | copy-start | bytes 1924
  6.5 72.0 %all-gather.4.cloned.1.call-start = ((), (), s32[]{:S(2)}) async-start(), calls=%async_computation | async-start | bytes 9338880 | tf_op jit(solution)/shard_map/all_gather | solution.py:71
  25.6 12.6 %copy-start.6 = (bf16[3,3,80,160]{3,2,1,0:T(8,128)(2,1)S(1)}, bf16[3,3,80,160]{3,2,1,0:T(8,128)(2,1)}, u32[]{:S(2)}) copy-start(bf16[3,3,80,160]{3,2,1,0:T(8,128)(2,1)} %param.12) | copy-start | bytes 691204
  25.6 6.1 %collective-permute-start = (bf16[2,1,160,128]{3,2,1,0:T(8,128)(2,1)S(1)}, bf16[2,1,160,128]{3,2,1,0:T(8,128)(2,1)S(1)}, u32[]{:S(2)}, u32[]{:S(2)}) collective-permute-start(bf16[2,1,160,128]{3,2,1,0:T(8,128)(2,1)S(1)} %get-tuple-element.7), channel_id=1, source_target_pairs={{0,2},{1,3},{4,6},{5,7},{8,10},{9,11},{12,14},{13,15},{16,18},{17,... | collective-permute-start | bytes 245768 | tf_op jit(solution)/shard_map/ppermute | solution.py:16
  29.7 6.3 %collective-permute-start.1 = (bf16[2,1,160,128]{3,2,1,0:T(8,128)(2,1)S(1)}, bf16[2,1,160,128]{3,2,1,0:T(8,128)(2,1)S(1)}, u32[]{:S(2)}, u32[]{:S(2)}) collective-permute-start(bf16[2,1,160,128]{3,2,1,0:T(8,128)(2,1)S(1)} %get-tuple-element.8), channel_id=1, source_target_pairs={{2,0},{3,1},{6,4},{7,5},{10,8},{11,9},{14,12},{15,13},{18,16},{19,... | collective-permute-start | bytes 245768 | tf_op jit(solution)/shard_map/ppermute | solution.py:19
  38.1 154.5 %all-gather.6.cloned.1.call-start = ((), (), s32[]{:S(2)}) async-start(), calls=%async_computation.1 | async-start | bytes 8847360 | tf_op jit(solution)/shard_map/all_gather | solution.py:92
  38.5 39.4 %copy-start.14 = (u32[32]{0:T(128)S(1)}, u32[32]{0:T(128)}, u32[]{:S(2)}) copy-start(u32[32]{0:T(128)} %constant.25) | copy-start | bytes 388
  78.5 4.6 %copy-start = (bf16[2,38,320,128]{3,2,1,0:T(8,128)(2,1)S(1)}, bf16[2,38,320,128]{3,2,1,0:T(8,128)(2,1)}, u32[]{:S(2)}) copy-start(bf16[2,38,320,128]{3,2,1,0:T(8,128)(2,1)} %all-gather.4.cloned.1.call-done) | copy-start | bytes 18677764
  96.2 4.4 %copy-start.3 = (bf16[1,1,320,160]{2,3,1,0:T(8,128)(2,1)S(1)}, bf16[1,1,320,160]{2,3,1,0:T(8,128)(2,1)}, u32[]{:S(2)}) copy-start(bf16[1,1,320,160]{2,3,1,0:T(8,128)(2,1)} %copy.61) | copy-start | bytes 307204
  100.6 4.2 %copy-start.4 = (bf16[1,1,320,160]{2,3,1,0:T(8,128)(2,1)S(1)}, bf16[1,1,320,160]{2,3,1,0:T(8,128)(2,1)}, u32[]{:S(2)}) copy-start(bf16[1,1,320,160]{2,3,1,0:T(8,128)(2,1)} %copy.58) | copy-start | bytes 307204
  104.8 4.4 %copy-start.5 = (bf16[1,1,320,160]{2,3,1,0:T(8,128)(2,1)S(1)}, bf16[1,1,320,160]{2,3,1,0:T(8,128)(2,1)}, u32[]{:S(2)}) copy-start(bf16[1,1,320,160]{2,3,1,0:T(8,128)(2,1)} %copy.55) | copy-start | bytes 307204
  109.3 4.2 %copy-start.8 = (f32[160]{0:T(256)S(1)}, f32[160]{0:T(256)}, u32[]{:S(2)}) copy-start(f32[160]{0:T(256)} %param.13) | copy-start | bytes 1924
  113.5 59.0 %copy-start.12 = (f32[160]{0:T(256)S(1)}, f32[160]{0:T(256)}, u32[]{:S(2)}) copy-start(f32[160]{0:T(256)} %param.15) | copy-start | bytes 1924
  113.5 59.0 %copy-start.13 = (f32[160]{0:T(256)S(1)}, f32[160]{0:T(256)}, u32[]{:S(2)}) copy-start(f32[160]{0:T(256)} %param.14) | copy-start | bytes 1924
  177.6 27.3 %copy-start.7 = (bf16[3,80,160]{2,1,0:T(8,128)(2,1)S(1)}, bf16[3,80,160]{2,1,0:T(8,128)(2,1)}, u32[]{:S(2)}) copy-start(bf16[3,80,160]{2,1,0:T(8,128)(2,1)} %param.16) | copy-start | bytes 230404
  198.2 92.3 %collective-permute-start.2 = (bf16[1,36,320,128]{3,2,1,0:T(8,128)(2,1)}, bf16[1,36,320,128]{3,2,1,0:T(8,128)(2,1)}, u32[]{:S(2)}, u32[]{:S(2)}) collective-permute-start(bf16[1,36,320,128]{3,2,1,0:T(8,128)(2,1)} %get-tuple-element.6), channel_id=1, source_target_pairs={{0,4},{4,8},{8,12},{1,5},{5,9},{9,13},{2,6},{6,10},{10,14},{3,7},{... | collective-permute-start | bytes 8847368 | tf_op jit(solution)/shard_map/ppermute | solution.py:16
  203.5 93.3 %collective-permute-start.3 = (bf16[1,36,320,128]{3,2,1,0:T(8,128)(2,1)}, bf16[1,36,320,128]{3,2,1,0:T(8,128)(2,1)}, u32[]{:S(2)}, u32[]{:S(2)}) collective-permute-start(bf16[1,36,320,128]{3,2,1,0:T(8,128)(2,1)} %get-tuple-element.5), channel_id=1, source_target_pairs={{4,0},{8,4},{12,8},{5,1},{9,5},{13,9},{6,2},{10,6},{14,10},{7,3},{... | collective-permute-start | bytes 8847368 | tf_op jit(solution)/shard_map/ppermute | solution.py:19
  285.8 4.8 %slice-start = ((s8[5898240]{0:T(1024)(128)(4,1)}), s8[1703936]{0:T(1024)(128)(4,1)S(1)}, s32[]{:S(2)}) async-start(s8[5898240]{0:T(1024)(128)(4,1)} %bitcast.94), calls=%async_computation.2 | async-start | bytes 3407872
  286.0 4.6 %slice-start.1 = ((s8[5898240]{0:T(1024)(128)(4,1)}), s8[4194304]{0:T(1024)(128)(4,1)S(1)}, s32[]{:S(2)}) async-start(s8[5898240]{0:T(1024)(128)(4,1)} %bitcast.94), calls=%async_computation.3 | async-start | bytes 8388608
  290.5 6.3 %copy-start.1 = (bf16[2,36,160,128]{3,2,1,0:T(8,128)(2,1)S(1)}, bf16[2,36,160,128]{3,2,1,0:T(8,128)(2,1)}, u32[]{:S(2)}) copy-start(bf16[2,36,160,128]{3,2,1,0:T(8,128)(2,1)} %get-tuple-element.22) | copy-start | bytes 8847364
  290.5 6.3 %copy-start.9 = (f32[160]{0:T(256)S(1)}, f32[160]{0:T(256)}, u32[]{:S(2)}) copy-start(f32[160]{0:T(256)} %param.17) | copy-start | bytes 1924
Sparse Core Ops, SparseCore 0:
  38.3 16.9 all-gather.3
  177.7 14.8 all-gather.5
